TPU v7x, 256 devices: a whole 4x4x8 slice. The times are simulated.
256 devices in a mesh: dp: 4 (over x), expert: 64 (over z, y, core).
Axes of the slice: x: 4, y: 4, z: 8, core: 2. Of those that a mesh axis runs over, the one named last changes fastest.
Arguments:
- hidden_in: bfloat16 [16384, 2048], P(('dp', 'expert')), may hold values from -6 to 6
- context: bfloat16 [16384, 2, 2048], P(('dp', 'expert')), may hold values from -6 to 6
- att_routes: int32 [16384, 2], P(('dp', 'expert')), may hold values from 0 to 7, all different within a row; in each aligned block of 64 rows (0 to 63, 64 to 127, ...) at most 20 rows name the same one
- att_logits: float32 [16384, 8], P(('dp', 'expert')), may hold values from -6 to 6
- ffn_routes: int32 [16384, 2], P(('dp', 'expert')), may hold values from 0 to 7, all different within a row; in each aligned block of 64 rows (0 to 63, 64 to 127, ...) at most 20 rows name the same one
- ffn_logits: float32 [16384, 8], P(('dp', 'expert')), may hold values from -6 to 6
- att_output_map: bfloat16 [64, 2048, 256], P('expert', 'dp'), may hold values from -0.125 to 0.125
- ffn_gate_up: bfloat16 [64, 2048, 2, 704], P('expert', 'dp'), may hold values from -0.125 to 0.125
- ffn_down: bfloat16 [64, 704, 2048], P('expert', None, 'dp'), may hold values from -0.078125 to 0.078125
- norm_gain: bfloat16 [2048], replicated, may hold values from 0.5 to 1.5
- out_gain: bfloat16 [2048], replicated, may hold values from 0.5 to 1.5
Outputs:
- layer_out: bfloat16 [16384, 2048], P(('dp', 'expert'))
Inputs may be any that keep to these rules, and one draw needn't show every extreme that they name: `att_routes`: the two ids of a row differ. In the rows of one device no attention expert is named more than 20 times, and on some device one is named exactly 20 times. `ffn_routes`: the two ids of a row differ. In the rows of one device no feed-forward expert is named more than 20 times, and on some device one is named exactly 20 times.
All inputs are finite; a program needn't handle non-finite values.
Results may differ from a plain program's by a relative error of at most 0.0054.
Values may be sent and summed in bfloat16 or wider, within the bound.
No kernel may reach another device: no remote copies, remote signals or barrier semaphores. Data moves between devices by JAX's collectives and lax.ppermute only.
A program may use at most 128 MiB of HBM per device.

v0:
```python
import jax
import jax.numpy as jnp
from jax import lax
from jax.sharding import Mesh
from jax.sharding import PartitionSpec as P

EXPERTS = 8
CAP = 20
CORES = 2


EPSILON = 1e-06


def norm_rows(values, gain):
    mean_square = jnp.mean(values * values, axis=-1, keepdims=True)
    return values * lax.rsqrt(mean_square + EPSILON) * gain.astype(jnp.float32)


def pair_weights(logits, routes):
    expert_ids = jnp.arange(logits.shape[1], dtype=jnp.int32)
    selected = routes[:, :, None] == expert_ids[None, None, :]
    chosen = jnp.sum(jnp.where(selected, logits[:, None, :], 0.0), axis=2)
    first_weight = jax.nn.sigmoid(chosen[:, 0] - chosen[:, 1])
    return jnp.stack([first_weight, 1.0 - first_weight], axis=1)


def slot_matrix(routes, capacity, experts):
    route_list = routes.reshape(-1)
    onehot = (route_list[:, None] == jnp.arange(experts, dtype=jnp.int32)[None, :]).astype(
        jnp.int32
    )
    before = jnp.cumsum(onehot, axis=0) - onehot
    slot_index = jnp.sum(before * onehot, axis=1)
    target = slot_index * experts + route_list
    slot_ids = jnp.arange(experts * capacity, dtype=jnp.int32)
    return slot_ids[:, None] == target[None, :]


def from_left(x):
    n = lax.axis_size("ey")
    return lax.ppermute(x, "ey", [(i, (i + 1) % n) for i in range(n)])


def from_right(x):
    n = lax.axis_size("ey")
    return lax.ppermute(x, "ey", [(i, (i - 1) % n) for i in range(n)])


def ring_copies(block):
    half = block.shape[0] // 2
    left = from_left(block)
    right = from_right(block)
    far = jnp.concatenate([from_left(left[:half]), from_right(right[half:])], axis=0)
    return jnp.stack([block, right, far, left], axis=0)


def ring_sums(parts):
    half = parts.shape[1] // 2
    far = parts[2].astype(jnp.bfloat16)
    early_right = from_right(far[:half]).astype(jnp.float32)
    early_left = from_left(far[half:]).astype(jnp.float32)
    to_left = jnp.concatenate([parts[3, :half] + early_right, parts[3, half:]], axis=0)
    to_right = jnp.concatenate([parts[1, :half], parts[1, half:] + early_left], axis=0)
    got_right = from_right(to_left.astype(jnp.bfloat16)).astype(jnp.float32)
    got_left = from_left(to_right.astype(jnp.bfloat16)).astype(jnp.float32)
    return parts[0] + got_right + got_left


def dispatch(blocks):
    arrived = lax.all_to_all(blocks, "ez", split_axis=1, concat_axis=1, tiled=True)
    return ring_copies(arrived)


def chip_pair(weights):
    return weights, lax.ppermute(weights, "ec", [(0, 1), (1, 0)])


def local(
    hidden_in,
    context,
    att_routes,
    att_logits,
    ffn_routes,
    ffn_logits,
    att_output_map,
    ffn_gate_up,
    ffn_down,
    norm_gain,
    out_gain,
):
    rows_dev = hidden_in.shape[0]
    model_width = hidden_in.shape[1]
    att_dim = context.shape[2]
    out_slice = att_output_map.shape[2]
    hid_slice = ffn_gate_up.shape[3]
    n_ez = lax.axis_size("ez")
    n_ey = lax.axis_size("ey")
    capacity = CAP

    att_matrix = lax.all_gather(att_output_map, "dp", axis=1, tiled=True)[0]
    gate_matrix = lax.all_gather(ffn_gate_up, "dp", axis=1, tiled=True)[0]
    down_matrix = lax.all_gather(ffn_down, "dp", axis=2, tiled=True)[0]
    att_own, att_other = chip_pair(att_matrix)
    core = lax.axis_index("ec")
    att_first = jnp.where(core == 0, att_own, att_other)
    att_second = jnp.where(core == 0, att_other, att_own)

    att_weight = pair_weights(att_logits, att_routes)
    att_place = slot_matrix(att_routes, capacity, EXPERTS)
    outgoing = jnp.dot(
        att_place.astype(jnp.bfloat16),
        context.reshape(-1, att_dim),
        preferred_element_type=jnp.float32,
    ).astype(jnp.bfloat16)
    incoming = dispatch(outgoing.reshape(capacity, EXPERTS, att_dim))
    rows_in = incoming.reshape(-1, att_dim)
    mapped = jnp.stack(
        [
            jnp.dot(rows_in, att_first, preferred_element_type=jnp.float32),
            jnp.dot(rows_in, att_second, preferred_element_type=jnp.float32),
        ],
        axis=1,
    ).astype(jnp.bfloat16)
    pair_width = CORES * out_slice
    mapped = mapped.reshape(n_ey, capacity, n_ez, pair_width)
    me = lax.axis_index("ey")
    twice = jnp.concatenate([mapped, mapped], axis=0)
    mapped = lax.dynamic_slice_in_dim(twice, (n_ey - me) % n_ey, n_ey, axis=0)
    mapped = jnp.transpose(mapped, (2, 0, 1, 3)).reshape(n_ez * n_ey, capacity, pair_width)
    back = lax.all_to_all(mapped, ("ez", "ey"), split_axis=0, concat_axis=0, tiled=True)
    back = back.reshape(EXPERTS, n_ey, capacity, pair_width)
    back = jnp.transpose(back, (2, 0, 1, 3)).reshape(capacity * EXPERTS, model_width)
    picked = jnp.dot(
        att_place.T.astype(jnp.bfloat16), back, preferred_element_type=jnp.float32
    )
    gate_matrix, _ = lax.optimization_barrier((gate_matrix, picked))
    depth = gate_matrix.shape[0]
    gate_own, gate_other = chip_pair(gate_matrix.reshape(depth, 2 * hid_slice))
    picked = picked.reshape(rows_dev, 2, model_width)
    hidden_state = (
        hidden_in.astype(jnp.float32)
        + att_weight[:, 0:1] * picked[:, 0]
        + att_weight[:, 1:2] * picked[:, 1]
    )
    ffn_in = norm_rows(hidden_state, norm_gain).astype(jnp.bfloat16)
    ffn_place = slot_matrix(ffn_routes, capacity, EXPERTS)
    row_place = jnp.any(ffn_place.reshape(EXPERTS * capacity, rows_dev, 2), axis=2)
    outgoing_rows = jnp.dot(
        row_place.astype(jnp.bfloat16), ffn_in, preferred_element_type=jnp.float32
    ).astype(jnp.bfloat16)
    incoming = dispatch(outgoing_rows.reshape(capacity, EXPERTS, model_width))
    flattened = incoming.reshape(-1, model_width)
    down_matrix, _ = lax.optimization_barrier((down_matrix, incoming))
    down_own, down_other = chip_pair(down_matrix)

    def slice_part(gate_w, down_w):
        gate_up = jnp.dot(flattened, gate_w, preferred_element_type=jnp.float32)
        gate_up = gate_up.reshape(-1, 2, hid_slice)
        activated = (jax.nn.silu(gate_up[:, 0]) * gate_up[:, 1]).astype(jnp.bfloat16)
        part = jnp.dot(activated, down_w, preferred_element_type=jnp.float32)
        return part.astype(jnp.bfloat16).astype(jnp.float32)

    projected = slice_part(gate_own, down_own) + slice_part(gate_other, down_other)
    reduced = projected.reshape(n_ey, capacity * n_ez, model_width)
    reduced = ring_sums(reduced).astype(jnp.bfloat16)
    reduced = reduced.reshape(capacity, n_ez, model_width)
    summed = lax.all_to_all(reduced, "ez", split_axis=1, concat_axis=1, tiled=True)
    summed = summed.reshape(capacity * EXPERTS, model_width).astype(jnp.float32)
    ffn_weight = pair_weights(ffn_logits, ffn_routes)
    weighted = ffn_place.astype(jnp.float32) * ffn_weight.reshape(1, -1)
    expert_mix = jnp.dot(weighted.T, summed, precision=lax.Precision.HIGHEST).reshape(
        rows_dev, 2, model_width
    )
    mixed_sum = hidden_state + (expert_mix[:, 0] + expert_mix[:, 1])
    return norm_rows(mixed_sum, out_gain).astype(jnp.bfloat16)


def solution(mesh):
    n_dp = mesh.devices.shape[0]
    n_expert = mesh.devices.shape[1]
    n_ey = n_expert // (EXPERTS * CORES)
    grid = Mesh(
        mesh.devices.reshape(n_dp, EXPERTS, n_ey, CORES), ("dp", "ez", "ey", "ec")
    )
    rows = ("dp", "ez", "ey", "ec")
    owners = ("ez", "ey", "ec")
    return jax.shard_map(
        local,
        mesh=grid,
        in_specs=(
            P(rows, None),
            P(rows, None, None),
            P(rows, None),
            P(rows, None),
            P(rows, None),
            P(rows, None),
            P(owners, "dp", None),
            P(owners, "dp", None, None),
            P(owners, None, "dp"),
            P(),
            P(),
        ),
        out_specs=P(rows, None),
        check_vma=False,
    )
```

profile of v0, /device:TPU:1, one launch (start us, length us, event | category | flops | bytes accessed | tf_op | source)
XLA Modules:
  0.0 260.2 jit_solution(4981084442990081420)
XLA Ops:
  11.3 30.4 %all_to_all.20 = bf16[20,8,2048]{2,0,1:T(8,128)(2,1)S(1)} all-to-all(bf16[20,8,2048]{2,0,1:T(8,128)(2,1)S(1)} %copy.129), channel_id=1, replica_groups=mesh['dp'=4,'ez'=8,'ey'=4,'ec'=2] {'ez'}, dimensions={1} | all-to-all | bytes 1310720 | tf_op jit(solution)/shard_map/all_to_all | solution.py:71
  45.0 2.9 %collective-permute-start.4 = (bf16[2048,256]{1,0:T(8,128)(2,1)}, bf16[2048,256]{1,0:T(8,128)(2,1)}, u32[]{:S(2)}, u32[]{:S(2)}) collective-permute-start(bf16[2048,256]{1,0:T(8,128)(2,1)} %bitcast.171), channel_id=1, source_target_pairs={{0,1},{1,0},{2,3},{3,2},{4,5},{5,4},{6,7},{7,6},{8,9},{9,8},{10,11... | collective-permute-start | bytes 3145736 | tf_op jit(solution)/shard_map/ppermute | solution.py:76
  47.9 9.4 %collective-permute-done.1 = bf16[20,8,2048]{2,1,0:T(8,128)(2,1)S(1)} collective-permute-done((bf16[20,8,2048]{2,1,0:T(8,128)(2,1)S(1)}, bf16[20,8,2048]{2,1,0:T(8,128)(2,1)S(1)}, u32[]{:S(2)}, u32[]{:S(2)}) %collective-permute-start.1) | collective-permute-done | bytes 655392 | tf_op jit(solution)/shard_map/ppermute | solution.py:42
  57.5 2.7 %collective-permute-start.3 = (bf16[10,8,2048]{2,1,0:T(8,128)(2,1)S(1)}, bf16[10,8,2048]{2,1,0:T(8,128)(2,1)S(1)}, u32[]{:S(2)}, u32[]{:S(2)}) collective-permute-start(bf16[10,8,2048]{2,1,0:T(8,128)(2,1)S(1)} %slice.101), channel_id=1, source_target_pairs={{0,6},{2,0},{4,2},{6,4},{1,7},{3,1},{5,3},{7,5},{8,14},{10,8},{12,... | collective-permute-start | bytes 983048 | tf_op jit(solution)/shard_map/ppermute | solution.py:47
  60.6 4.4 %collective-permute-done.2 = bf16[10,8,2048]{2,1,0:T(8,128)(2,1)S(1)} collective-permute-done((bf16[10,8,2048]{2,1,0:T(8,128)(2,1)S(1)}, bf16[10,8,2048]{2,1,0:T(8,128)(2,1)S(1)}, u32[]{:S(2)}, u32[]{:S(2)}) %collective-permute-start.2) | collective-permute-done | bytes 327712 | tf_op jit(solution)/shard_map/ppermute | solution.py:42
  66.2 2.1 fusion.10
  71.9 7.8 %all-to-all-start.1 = ((bf16[32,20,512]{2,1,0:T(8,128)(2,1)}), bf16[32,20,512]{2,1,0:T(8,128)(2,1)S(1)}, u32[]{:S(2)}, u32[]{:S(2)}) async-start(bf16[32,20,512]{2,1,0:T(8,128)(2,1)} %bitcast.11), calls=%async_computation.1 | async-start | bytes 1572864 | tf_op jit(solution)/shard_map/all_to_all | solution.py:131
  81.3 16.7 %all-to-all-done.1 = bf16[32,20,512]{2,1,0:T(8,128)(2,1)S(1)} async-done(((bf16[32,20,512]{2,1,0:T(8,128)(2,1)}), bf16[32,20,512]{2,1,0:T(8,128)(2,1)S(1)}, u32[]{:S(2)}, u32[]{:S(2)}) %all-to-all-start.1) | async-done | bytes 655392 | tf_op jit(solution)/shard_map/all_to_all | solution.py:131
  98.9 6.7 %all-gather.6.cloned.1.call-done = bf16[1,2048,2,704]{1,3,2,0:T(8,128)(2,1)} async-done(((bf16[1,512,2,704]{1,3,2,0:T(8,128)(2,1)}), bf16[1,2048,2,704]{1,3,2,0:T(8,128)(2,1)}) %all-gather.6.cloned.1.call-update) | async-done | bytes 5767184 | tf_op jit(solution)/shard_map/all_gather | solution.py:102
  109.0 30.1 %all_to_all.21 = bf16[20,8,2048]{2,0,1:T(8,128)(2,1)S(1)} all-to-all(bf16[20,8,2048]{2,0,1:T(8,128)(2,1)S(1)} %copy.141), channel_id=1, replica_groups=mesh['dp'=4,'ez'=8,'ey'=4,'ec'=2] {'ez'}, dimensions={1} | all-to-all | bytes 1310720 | tf_op jit(solution)/shard_map/all_to_all | solution.py:71
  142.3 14.4 %collective-permute-done.6 = bf16[20,8,2048]{2,1,0:T(8,128)(2,1)S(1)} collective-permute-done((bf16[20,8,2048]{2,1,0:T(8,128)(2,1)S(1)}, bf16[20,8,2048]{2,1,0:T(8,128)(2,1)S(1)}, u32[]{:S(2)}, u32[]{:S(2)}) %collective-permute-start.6) | collective-permute-done | bytes 655392 | tf_op jit(solution)/shard_map/ppermute | solution.py:42
  157.2 2.7 %collective-permute-start.8 = (bf16[10,8,2048]{2,0,1:T(8,128)(2,1)S(1)}, bf16[10,8,2048]{2,0,1:T(8,128)(2,1)S(1)}, u32[]{:S(2)}, u32[]{:S(2)}) collective-permute-start(bf16[10,8,2048]{2,0,1:T(8,128)(2,1)S(1)} %copy.175), channel_id=1, source_target_pairs={{0,6},{2,0},{4,2},{6,4},{1,7},{3,1},{5,3},{7,5},{8,14},{10,8},{12,... | collective-permute-start | bytes 983048 | tf_op jit(solution)/shard_map/ppermute | solution.py:47
  160.7 9.6 %collective-permute-done.7 = bf16[10,8,2048]{2,0,1:T(8,128)(2,1)S(1)} collective-permute-done((bf16[10,8,2048]{2,0,1:T(8,128)(2,1)S(1)}, bf16[10,8,2048]{2,0,1:T(8,128)(2,1)S(1)}, u32[]{:S(2)}, u32[]{:S(2)}) %collective-permute-start.7) | collective-permute-done | bytes 327712 | tf_op jit(solution)/shard_map/ppermute | solution.py:42
  171.1 2.5 collective-permute-start.10
  175.1 6.9 %fusion = f32[640,2,704]{0,2,1:T(8,128)S(1)} fusion(bf16[640,2048,1]{1,0,2:T(8,128)(2,1)S(1)} %bitcast.161, bf16[2048,2,704]{0,2,1:T(8,128)(2,1)} %bitcast.168), kind=kOutput, calls=%fused_computation | convolution fusion | flops 3690987520 | bytes 11993088 | tf_op jit(solution)/shard_map/dot_general | solution.py:158
  182.0 2.3 convolution_convert_fusion.1
  184.4 6.8 %fusion.58 = f32[640,2,704]{0,2,1:T(8,128)S(1)} fusion(bf16[640,2048,1]{1,0,2:T(8,128)(2,1)S(1)} %bitcast.162, bf16[2,704,2048]{2,1,0:T(8,128)(2,1)} %bitcast.34), kind=kOutput, calls=%fused_computation.110 | convolution fusion | flops 3690987520 | bytes 11993088 | tf_op jit(solution)/shard_map/dot_general | solution.py:158
  191.1 2.4 fusion.57
  194.0 3.1 %collective-permute-start.11 = (bf16[80,2048]{1,0:T(8,128)(2,1)S(1)}, bf16[80,2048]{1,0:T(8,128)(2,1)S(1)}, u32[]{:S(2)}, u32[]{:S(2)}) collective-permute-start(bf16[80,2048]{1,0:T(8,128)(2,1)S(1)} %get-tuple-element.17), channel_id=1, source_target_pairs={{0,6},{2,0},{4,2},{6,4},{1,7},{3,1},{5,3},{7,5},{8,14},{10,8},{12,... | collective-permute-start | bytes 983048 | tf_op jit(solution)/shard_map/ppermute | solution.py:47
  197.1 7.1 %collective-permute-done.11 = bf16[80,2048]{1,0:T(8,128)(2,1)S(1)} collective-permute-done((bf16[80,2048]{1,0:T(8,128)(2,1)S(1)}, bf16[80,2048]{1,0:T(8,128)(2,1)S(1)}, u32[]{:S(2)}, u32[]{:S(2)}) %collective-permute-start.11) | collective-permute-done | bytes 327712 | tf_op jit(solution)/shard_map/ppermute | solution.py:47
  204.2 3.1 %collective-permute-done.13 = bf16[80,2048]{1,0:T(8,128)(2,1)S(1)} collective-permute-done((bf16[80,2048]{1,0:T(8,128)(2,1)S(1)}, bf16[80,2048]{1,0:T(8,128)(2,1)S(1)}, u32[]{:S(2)}, u32[]{:S(2)}) %collective-permute-start.13) | collective-permute-done | bytes 327712 | tf_op jit(solution)/shard_map/ppermute | solution.py:42
  209.4 13.5 %collective-permute-done.12 = bf16[160,2048]{1,0:T(8,128)(2,1)S(1)} collective-permute-done((bf16[160,2048]{1,0:T(8,128)(2,1)S(1)}, bf16[160,2048]{1,0:T(8,128)(2,1)S(1)}, u32[]{:S(2)}, u32[]{:S(2)}) %collective-permute-start.12) | collective-permute-done | bytes 655392 | tf_op jit(solution)/shard_map/ppermute | solution.py:47
  226.2 3.5 %all-to-all-start.3 = ((bf16[20,8,2048]{2,0,1:T(8,128)(2,1)}), bf16[20,8,2048]{2,0,1:T(8,128)(2,1)S(1)}, u32[]{:S(2)}, u32[]{:S(2)}) async-start(bf16[20,8,2048]{2,0,1:T(8,128)(2,1)} %copy.149), calls=%async_computation.3 | async-start | bytes 1572864 | tf_op jit(solution)/shard_map/all_to_all | solution.py:168
  229.8 21.9 %all-to-all-done.3 = bf16[20,8,2048]{2,0,1:T(8,128)(2,1)S(1)} async-done(((bf16[20,8,2048]{2,0,1:T(8,128)(2,1)}), bf16[20,8,2048]{2,0,1:T(8,128)(2,1)S(1)}, u32[]{:S(2)}, u32[]{:S(2)}) %all-to-all-start.3) | async-done | bytes 655392 | tf_op jit(solution)/shard_map/all_to_all | solution.py:168
  (117 shorter events, 33.6 us)
Async XLA Ops:
  6.5 38.5 %all-gather.4.cloned.1.call-start = ((), (), s32[]{:S(2)}) async-start(), calls=%async_computation.4 | async-start | bytes 1310720 | tf_op jit(solution)/shard_map/all_gather | solution.py:101
  7.3 98.3 %all-gather.6.cloned.1.call-start = ((), (), s32[]{:S(2)}) async-start(), calls=%async_computation.5 | async-start | bytes 7208960 | tf_op jit(solution)/shard_map/all_gather | solution.py:102
  42.1 15.2 %collective-permute-start.1 = (bf16[20,8,2048]{2,1,0:T(8,128)(2,1)S(1)}, bf16[20,8,2048]{2,1,0:T(8,128)(2,1)S(1)}, u32[]{:S(2)}, u32[]{:S(2)}) collective-permute-start(bf16[20,8,2048]{2,1,0:T(8,128)(2,1)S(1)} %copy.130), channel_id=1, source_target_pairs={{0,2},{2,4},{4,6},{6,0},{1,3},{3,5},{5,7},{7,1},{8,10},{10,12},{12... | collective-permute-start | bytes 1966088 | tf_op jit(solution)/shard_map/ppermute | solution.py:42
  43.5 13.9 %collective-permute-start = (bf16[20,8,2048]{2,1,0:T(8,128)(2,1)S(1)}, bf16[20,8,2048]{2,1,0:T(8,128)(2,1)S(1)}, u32[]{:S(2)}, u32[]{:S(2)}) collective-permute-start(bf16[20,8,2048]{2,1,0:T(8,128)(2,1)S(1)} %copy.130), channel_id=1, source_target_pairs={{0,6},{2,0},{4,2},{6,4},{1,7},{3,1},{5,3},{7,5},{8,14},{10,8},{12,... | collective-permute-start | bytes 1966088 | tf_op jit(solution)/shard_map/ppermute | solution.py:47
  45.0 20.3 %collective-permute-start.4 = (bf16[2048,256]{1,0:T(8,128)(2,1)}, bf16[2048,256]{1,0:T(8,128)(2,1)}, u32[]{:S(2)}, u32[]{:S(2)}) collective-permute-start(bf16[2048,256]{1,0:T(8,128)(2,1)} %bitcast.171), channel_id=1, source_target_pairs={{0,1},{1,0},{2,3},{3,2},{4,5},{5,4},{6,7},{7,6},{8,9},{9,8},{10,11... | collective-permute-start | bytes 3145736 | tf_op jit(solution)/shard_map/ppermute | solution.py:76
  57.3 7.6 %collective-permute-start.2 = (bf16[10,8,2048]{2,1,0:T(8,128)(2,1)S(1)}, bf16[10,8,2048]{2,1,0:T(8,128)(2,1)S(1)}, u32[]{:S(2)}, u32[]{:S(2)}) collective-permute-start(bf16[10,8,2048]{2,1,0:T(8,128)(2,1)S(1)} %slice.100), channel_id=1, source_target_pairs={{0,2},{2,4},{4,6},{6,0},{1,3},{3,5},{5,7},{7,1},{8,10},{10,12},{12... | collective-permute-start | bytes 983048 | tf_op jit(solution)/shard_map/ppermute | solution.py:42
  57.5 7.5 %collective-permute-start.3 = (bf16[10,8,2048]{2,1,0:T(8,128)(2,1)S(1)}, bf16[10,8,2048]{2,1,0:T(8,128)(2,1)S(1)}, u32[]{:S(2)}, u32[]{:S(2)}) collective-permute-start(bf16[10,8,2048]{2,1,0:T(8,128)(2,1)S(1)} %slice.101), channel_id=1, source_target_pairs={{0,6},{2,0},{4,2},{6,4},{1,7},{3,1},{5,3},{7,5},{8,14},{10,8},{12,... | collective-permute-start | bytes 983048 | tf_op jit(solution)/shard_map/ppermute | solution.py:47
  71.9 26.2 %all-to-all-start.1 = ((bf16[32,20,512]{2,1,0:T(8,128)(2,1)}), bf16[32,20,512]{2,1,0:T(8,128)(2,1)S(1)}, u32[]{:S(2)}, u32[]{:S(2)}) async-start(bf16[32,20,512]{2,1,0:T(8,128)(2,1)} %bitcast.11), calls=%async_computation.1 | async-start | bytes 1572864 | tf_op jit(solution)/shard_map/all_to_all | solution.py:131
  79.6 91.5 %all-gather.8.cloned.1.call-start = ((), (), s32[]{:S(2)}) async-start(), calls=%async_computation.6 | async-start | bytes 3604480 | tf_op jit(solution)/shard_map/all_gather | solution.py:103
  80.4 25.9 %copy-start.4 = (bf16[2048]{0:T(1024)(128)(2,1)S(1)}, bf16[2048]{0:T(1024)(128)(2,1)}, u32[]{:S(2)}) copy-start(bf16[2048]{0:T(1024)(128)(2,1)} %param.20) | copy-start | bytes 12292
  105.5 78.8 %collective-permute-start.9 = (bf16[2048,1408]{0,1:T(8,128)(2,1)}, bf16[2048,1408]{0,1:T(8,128)(2,1)}, u32[]{:S(2)}, u32[]{:S(2)}) collective-permute-start(bf16[2048,1408]{0,1:T(8,128)(2,1)} %bitcast.167), channel_id=1, source_target_pairs={{0,1},{1,0},{2,3},{3,2},{4,5},{5,4},{6,7},{7,6},{8,9},{9,8},{10,11... | collective-permute-start | bytes 17301512 | tf_op jit(solution)/shard_map/ppermute | solution.py:76
  108.2 31.3 %copy-start = (f32[64,2048]{1,0:T(8,128)}, f32[64,2048]{1,0:T(8,128)S(1)}, u32[]{:S(2)}) copy-start(f32[64,2048]{1,0:T(8,128)S(1)} %get-tuple-element.12) | copy-start | bytes 1572868
  139.5 17.1 %collective-permute-start.6 = (bf16[20,8,2048]{2,1,0:T(8,128)(2,1)S(1)}, bf16[20,8,2048]{2,1,0:T(8,128)(2,1)S(1)}, u32[]{:S(2)}, u32[]{:S(2)}) collective-permute-start(bf16[20,8,2048]{2,1,0:T(8,128)(2,1)S(1)} %copy.142), channel_id=1, source_target_pairs={{0,2},{2,4},{4,6},{6,0},{1,3},{3,5},{5,7},{7,1},{8,10},{10,12},{12... | collective-permute-start | bytes 1966088 | tf_op jit(solution)/shard_map/ppermute | solution.py:42
  140.8 16.2 %collective-permute-start.5 = (bf16[20,8,2048]{2,1,0:T(8,128)(2,1)S(1)}, bf16[20,8,2048]{2,1,0:T(8,128)(2,1)S(1)}, u32[]{:S(2)}, u32[]{:S(2)}) collective-permute-start(bf16[20,8,2048]{2,1,0:T(8,128)(2,1)S(1)} %copy.142), channel_id=1, source_target_pairs={{0,6},{2,0},{4,2},{6,4},{1,7},{3,1},{5,3},{7,5},{8,14},{10,8},{12,... | collective-permute-start | bytes 1966088 | tf_op jit(solution)/shard_map/ppermute | solution.py:47
  156.9 13.4 %collective-permute-start.7 = (bf16[10,8,2048]{2,0,1:T(8,128)(2,1)S(1)}, bf16[10,8,2048]{2,0,1:T(8,128)(2,1)S(1)}, u32[]{:S(2)}, u32[]{:S(2)}) collective-permute-start(bf16[10,8,2048]{2,0,1:T(8,128)(2,1)S(1)} %copy.176), channel_id=1, source_target_pairs={{0,2},{2,4},{4,6},{6,0},{1,3},{3,5},{5,7},{7,1},{8,10},{10,12},{12... | collective-permute-start | bytes 983048 | tf_op jit(solution)/shard_map/ppermute | solution.py:42
  157.2 13.1 %collective-permute-start.8 = (bf16[10,8,2048]{2,0,1:T(8,128)(2,1)S(1)}, bf16[10,8,2048]{2,0,1:T(8,128)(2,1)S(1)}, u32[]{:S(2)}, u32[]{:S(2)}) collective-permute-start(bf16[10,8,2048]{2,0,1:T(8,128)(2,1)S(1)} %copy.175), channel_id=1, source_target_pairs={{0,6},{2,0},{4,2},{6,4},{1,7},{3,1},{5,3},{7,5},{8,14},{10,8},{12,... | collective-permute-start | bytes 983048 | tf_op jit(solution)/shard_map/ppermute | solution.py:47
  171.1 20.0 %collective-permute-start.10 = (bf16[704,2048]{1,0:T(8,128)(2,1)}, bf16[704,2048]{1,0:T(8,128)(2,1)S(1)}, u32[]{:S(2)}, u32[]{:S(2)}) collective-permute-start(bf16[704,2048]{1,0:T(8,128)(2,1)} %bitcast.169), channel_id=1, source_target_pairs={{0,1},{1,0},{2,3},{3,2},{4,5},{5,4},{6,7},{7,6},{8,9},{9,8},{10,11... | collective-permute-start | bytes 8650760 | tf_op jit(solution)/shard_map/ppermute | solution.py:76
  194.0 10.2 %collective-permute-start.11 = (bf16[80,2048]{1,0:T(8,128)(2,1)S(1)}, bf16[80,2048]{1,0:T(8,128)(2,1)S(1)}, u32[]{:S(2)}, u32[]{:S(2)}) collective-permute-start(bf16[80,2048]{1,0:T(8,128)(2,1)S(1)} %get-tuple-element.17), channel_id=1, source_target_pairs={{0,6},{2,0},{4,2},{6,4},{1,7},{3,1},{5,3},{7,5},{8,14},{10,8},{12,... | collective-permute-start | bytes 983048 | tf_op jit(solution)/shard_map/ppermute | solution.py:47
  197.0 10.2 %collective-permute-start.13 = (bf16[80,2048]{1,0:T(8,128)(2,1)S(1)}, bf16[80,2048]{1,0:T(8,128)(2,1)S(1)}, u32[]{:S(2)}, u32[]{:S(2)}) collective-permute-start(bf16[80,2048]{1,0:T(8,128)(2,1)S(1)} %get-tuple-element.18), channel_id=1, source_target_pairs={{0,2},{2,4},{4,6},{6,0},{1,3},{3,5},{5,7},{7,1},{8,10},{10,12},{12... | collective-permute-start | bytes 983048 | tf_op jit(solution)/shard_map/ppermute | solution.py:42
  207.5 15.5 %collective-permute-start.12 = (bf16[160,2048]{1,0:T(8,128)(2,1)S(1)}, bf16[160,2048]{1,0:T(8,128)(2,1)S(1)}, u32[]{:S(2)}, u32[]{:S(2)}) collective-permute-start(bf16[160,2048]{1,0:T(8,128)(2,1)S(1)} %pad_maximum_fusion.3), channel_id=1, source_target_pairs={{0,6},{2,0},{4,2},{6,4},{1,7},{3,1},{5,3},{7,5},{8,14},{10,8},{12,... | collective-permute-start | bytes 1966088 | tf_op jit(solution)/shard_map/ppermute | solution.py:47
  208.2 21.6 %copy-start.7 = (f32[64,8]{0,1:T(8,128)S(1)}, f32[64,8]{0,1:T(8,128)}, u32[]{:S(2)}) copy-start(f32[64,8]{0,1:T(8,128)} %param.16) | copy-start | bytes 6148
  208.2 16.4 %collective-permute-start.14 = (bf16[160,2048]{1,0:T(8,128)(2,1)S(1)}, bf16[160,2048]{1,0:T(8,128)(2,1)S(1)}, u32[]{:S(2)}, u32[]{:S(2)}) collective-permute-start(bf16[160,2048]{1,0:T(8,128)(2,1)S(1)} %pad_maximum_fusion.4), channel_id=1, source_target_pairs={{0,2},{2,4},{4,6},{6,0},{1,3},{3,5},{5,7},{7,1},{8,10},{10,12},{12... | collective-permute-start | bytes 1966088 | tf_op jit(solution)/shard_map/ppermute | solution.py:42
  224.9 27.7 %copy-start.1 = (f32[64,2048]{1,0:T(8,128)S(1)}, f32[64,2048]{1,0:T(8,128)}, u32[]{:S(2)}) copy-start(f32[64,2048]{1,0:T(8,128)} %copy-done) | copy-start | bytes 1572868
  226.2 25.5 %all-to-all-start.3 = ((bf16[20,8,2048]{2,0,1:T(8,128)(2,1)}), bf16[20,8,2048]{2,0,1:T(8,128)(2,1)S(1)}, u32[]{:S(2)}, u32[]{:S(2)}) async-start(bf16[20,8,2048]{2,0,1:T(8,128)(2,1)} %copy.149), calls=%async_computation.3 | async-start | bytes 1572864 | tf_op jit(solution)/shard_map/all_to_all | solution.py:168
  (7 other events, 70.6 us)
Sparse Core Ops, SparseCore 0:
  9.2 29.3 all-gather.3
  40.4 65.0 all-gather.5
  107.3 40.4 all-gather.7
where the time goes:
time: 261 us; the launch traced here: 260 us
  waiting for transfers between devices  110 us (42%)
  blocking collectives  60.5 us (23%)
  starting transfers between devices  33.7 us (13%)
  matrix products  23.4 us (9%)
  between operations  13.7 us (5%)
  local copies, waits for them, and re-layouts  13.5 us (5%)
  other arithmetic  4.91 us (2%)
    all_to_all x2, blocking collectives, dispatch(): lax.all_to_all(blocks, 'ez', split_axis=1, concat_axis=1, tiled=True)  60.5 us
    ppermute x6, waiting for transfers between devices, from_left(): return lax.ppermute(x, 'ey', [(i, (i + 1) % n) for i in range(n)])  42.6 us
    all_to_all x1, waiting for transfers between devices, local(): lax.all_to_all(reduced, 'ez', split_axis=1, concat_axis=1, tiled=True)  21.9 us
    ppermute x6, waiting for transfers between devices, from_right(): return lax.ppermute(x, 'ey', [(i, (i - 1) % n) for i in range(n)])  20.6 us
    all_to_all x1, waiting for transfers between devices, local(): lax.all_to_all(mapped, ('ez', 'ey'), split_axis=0, concat_axis=0, tiled=T...  16.7 us
    dot_general x2, matrix products, slice_part(): gate_up = jnp.dot(flattened, gate_w, preferred_element_type=jnp.float32)  13.7 us
    ppermute x6, starting transfers between devices, from_right(): return lax.ppermute(x, 'ey', [(i, (i - 1) % n) for i in range(n)])  12.2 us
    all_to_all x1, starting transfers between devices, local(): lax.all_to_all(mapped, ('ez', 'ey'), split_axis=0, concat_axis=0, tiled=T...  7.76 us
  transfers between devices with their start and end apart: 20, of which 11 were waited for; matrix products, arithmetic and copies ran while one was open for 13% of the time, Pallas kernels for 0%

commit v1 on v0

--- a/solution.py
+++ b/solution.py
@@ -134,9 +134,6 @@
     picked = jnp.dot(
         att_place.T.astype(jnp.bfloat16), back, preferred_element_type=jnp.float32
     )
-    gate_matrix, _ = lax.optimization_barrier((gate_matrix, picked))
-    depth = gate_matrix.shape[0]
-    gate_own, gate_other = chip_pair(gate_matrix.reshape(depth, 2 * hid_slice))
     picked = picked.reshape(rows_dev, 2, model_width)
     hidden_state = (
         hidden_in.astype(jnp.float32)
@@ -149,7 +146,17 @@
     outgoing_rows = jnp.dot(
         row_place.astype(jnp.bfloat16), ffn_in, preferred_element_type=jnp.float32
     ).astype(jnp.bfloat16)
-    incoming = dispatch(outgoing_rows.reshape(capacity, EXPERTS, model_width))
+    arrived = lax.all_to_all(
+        outgoing_rows.reshape(capacity, EXPERTS, model_width),
+        "ez",
+        split_axis=1,
+        concat_axis=1,
+        tiled=True,
+    )
+    gate_matrix, _ = lax.optimization_barrier((gate_matrix, arrived))
+    depth = gate_matrix.shape[0]
+    gate_own, gate_other = chip_pair(gate_matrix.reshape(depth, 2 * hid_slice))
+    incoming = ring_copies(arrived)
     flattened = incoming.reshape(-1, model_width)
     down_matrix, _ = lax.optimization_barrier((down_matrix, incoming))
     down_own, down_other = chip_pair(down_matrix)

time: 261 us -> 254 us (0.973)
  blocking collectives: 60.5 us -> 30.4 us
  waiting for transfers between devices: 110 us -> 123 us
  starting transfers between devices: 33.7 us -> 42.1 us
    all_to_all x2 -> x1, blocking collectives: 60.5 us -> 30.4 us  [dispatch(): lax.all_to_all(blocks, 'ez', split_axis=1, concat_axis=1, tiled=True)]
    all_to_all x0 -> x1, waiting for transfers between devices: none -> 17.4 us  [local(): lax.all_to_all(outgoing_rows.reshape(capacity, EXPERTS, model_width), 'ez...]
    all_gather x1, waiting for transfers between devices: 6.65 us -> 0.01 us  [local(): gate_matrix = lax.all_gather(ffn_gate_up, 'dp', axis=1, tiled=True)[0]]
    ppermute x3, starting transfers between devices: 6.08 us -> 10.6 us  [chip_pair(): return (weights, lax.ppermute(weights, 'ec', [(0, 1), (1, 0)]))]
    all_to_all x0 -> x1, starting transfers between devices: none -> 3.55 us  [local(): lax.all_to_all(outgoing_rows.reshape(capacity, EXPERTS, model_width), 'ez...]
  transfers between devices with their start and end apart: 20 -> 21, of which waited for: 11 -> 11; matrix products, arithmetic and copies ran while one was open for 13% -> 14% of each run, Pallas kernels for 0% -> 0%
where the time goes in v1:
time: 254 us; the launch traced here: 252 us
  waiting for transfers between devices  123 us (48%)
  starting transfers between devices  42.1 us (17%)
  blocking collectives  30.4 us (12%)
  matrix products  23.3 us (9%)
  local copies, waits for them, and re-layouts  14.1 us (6%)
  between operations  13.7 us (5%)
  other arithmetic  5.79 us (2%)
    ppermute x6, waiting for transfers between devices, from_left(): return lax.ppermute(x, 'ey', [(i, (i + 1) % n) for i in range(n)])  44 us
    all_to_all x1, blocking collectives, dispatch(): lax.all_to_all(blocks, 'ez', split_axis=1, concat_axis=1, tiled=True)  30.4 us
    all_to_all x1, waiting for transfers between devices, local(): lax.all_to_all(reduced, 'ez', split_axis=1, concat_axis=1, tiled=True)  21.9 us
    ppermute x6, waiting for transfers between devices, from_right(): return lax.ppermute(x, 'ey', [(i, (i - 1) % n) for i in range(n)])  20.6 us
    all_to_all x1, waiting for transfers between devices, local(): lax.all_to_all(outgoing_rows.reshape(capacity, EXPERTS, model_width), 'ez...  17.4 us
    all_to_all x1, waiting for transfers between devices, local(): lax.all_to_all(mapped, ('ez', 'ey'), split_axis=0, concat_axis=0, tiled=T...  17 us
    dot_general x2, matrix products, slice_part(): gate_up = jnp.dot(flattened, gate_w, preferred_element_type=jnp.float32)  13.7 us
    ppermute x6, starting transfers between devices, from_right(): return lax.ppermute(x, 'ey', [(i, (i - 1) % n) for i in range(n)])  12.2 us
  transfers between devices with their start and end apart: 21, of which 11 were waited for; matrix products, arithmetic and copies ran while one was open for 14% of the time, Pallas kernels for 0%

profile of v1, /device:TPU:1, one launch (start us, length us, event | category | flops | bytes accessed | tf_op | source)
XLA Modules:
  0.0 252.4 jit_solution(14173787513060377377)
XLA Ops:
  11.3 30.4 %all_to_all.20 = bf16[20,8,2048]{2,0,1:T(8,128)(2,1)S(1)} all-to-all(bf16[20,8,2048]{2,0,1:T(8,128)(2,1)S(1)} %copy.122), channel_id=1, replica_groups=mesh['dp'=4,'ez'=8,'ey'=4,'ec'=2] {'ez'}, dimensions={1} | all-to-all | bytes 1310720 | tf_op jit(solution)/shard_map/all_to_all | solution.py:71
  45.0 2.9 %collective-permute-start.4 = (bf16[2048,256]{1,0:T(8,128)(2,1)}, bf16[2048,256]{1,0:T(8,128)(2,1)}, u32[]{:S(2)}, u32[]{:S(2)}) collective-permute-start(bf16[2048,256]{1,0:T(8,128)(2,1)} %bitcast.167), channel_id=1, source_target_pairs={{0,1},{1,0},{2,3},{3,2},{4,5},{5,4},{6,7},{7,6},{8,9},{9,8},{10,11... | collective-permute-start | bytes 3145736 | tf_op jit(solution)/shard_map/ppermute | solution.py:76
  47.9 9.4 %collective-permute-done.1 = bf16[20,8,2048]{2,1,0:T(8,128)(2,1)S(1)} collective-permute-done((bf16[20,8,2048]{2,1,0:T(8,128)(2,1)S(1)}, bf16[20,8,2048]{2,1,0:T(8,128)(2,1)S(1)}, u32[]{:S(2)}, u32[]{:S(2)}) %collective-permute-start.1) | collective-permute-done | bytes 655392 | tf_op jit(solution)/shard_map/ppermute | solution.py:42
  57.5 2.7 %collective-permute-start.3 = (bf16[10,8,2048]{2,1,0:T(8,128)(2,1)S(1)}, bf16[10,8,2048]{2,1,0:T(8,128)(2,1)S(1)}, u32[]{:S(2)}, u32[]{:S(2)}) collective-permute-start(bf16[10,8,2048]{2,1,0:T(8,128)(2,1)S(1)} %slice.101), channel_id=1, source_target_pairs={{0,6},{2,0},{4,2},{6,4},{1,7},{3,1},{5,3},{7,5},{8,14},{10,8},{12,... | collective-permute-start | bytes 983048 | tf_op jit(solution)/shard_map/ppermute | solution.py:47
  60.6 4.4 %collective-permute-done.2 = bf16[10,8,2048]{2,1,0:T(8,128)(2,1)S(1)} collective-permute-done((bf16[10,8,2048]{2,1,0:T(8,128)(2,1)S(1)}, bf16[10,8,2048]{2,1,0:T(8,128)(2,1)S(1)}, u32[]{:S(2)}, u32[]{:S(2)}) %collective-permute-start.2) | collective-permute-done | bytes 327712 | tf_op jit(solution)/shard_map/ppermute | solution.py:42
  66.2 2.1 fusion.10
  71.8 7.9 %all-to-all-start.1 = ((bf16[32,20,512]{2,1,0:T(8,128)(2,1)}), bf16[32,20,512]{2,1,0:T(8,128)(2,1)S(1)}, u32[]{:S(2)}, u32[]{:S(2)}) async-start(bf16[32,20,512]{2,1,0:T(8,128)(2,1)} %bitcast.11), calls=%async_computation.1 | async-start | bytes 1572864 | tf_op jit(solution)/shard_map/all_to_all | solution.py:131
  81.0 17.0 %all-to-all-done.1 = bf16[32,20,512]{2,1,0:T(8,128)(2,1)S(1)} async-done(((bf16[32,20,512]{2,1,0:T(8,128)(2,1)}), bf16[32,20,512]{2,1,0:T(8,128)(2,1)S(1)}, u32[]{:S(2)}, u32[]{:S(2)}) %all-to-all-start.1) | async-done | bytes 655392 | tf_op jit(solution)/shard_map/all_to_all | solution.py:131
  102.0 3.6 %all-to-all-start.2 = ((bf16[20,8,2048]{2,0,1:T(8,128)(2,1)}), bf16[20,8,2048]{2,0,1:T(8,128)(2,1)S(1)}, u32[]{:S(2)}, u32[]{:S(2)}) async-start(bf16[20,8,2048]{2,0,1:T(8,128)(2,1)} %copy.133), calls=%async_computation.2 | async-start | bytes 1572864 | tf_op jit(solution)/shard_map/all_to_all | solution.py:149
  106.2 17.4 %all-to-all-done.2 = bf16[20,8,2048]{2,0,1:T(8,128)(2,1)S(1)} async-done(((bf16[20,8,2048]{2,0,1:T(8,128)(2,1)}), bf16[20,8,2048]{2,0,1:T(8,128)(2,1)S(1)}, u32[]{:S(2)}, u32[]{:S(2)}) %all-to-all-start.2) | async-done | bytes 655392 | tf_op jit(solution)/shard_map/all_to_all | solution.py:149
  123.6 6.0 %collective-permute-start.9 = (bf16[2048,1408]{0,1:T(8,128)(2,1)}, bf16[2048,1408]{0,1:T(8,128)(2,1)}, u32[]{:S(2)}, u32[]{:S(2)}) collective-permute-start(bf16[2048,1408]{0,1:T(8,128)(2,1)} %bitcast.163), channel_id=1, source_target_pairs={{0,1},{1,0},{2,3},{3,2},{4,5},{5,4},{6,7},{7,6},{8,9},{9,8},{10,11... | collective-permute-start | bytes 17301512 | tf_op jit(solution)/shard_map/ppermute | solution.py:76
  132.9 15.0 %collective-permute-done.6 = bf16[20,8,2048]{2,1,0:T(8,128)(2,1)S(1)} collective-permute-done((bf16[20,8,2048]{2,1,0:T(8,128)(2,1)S(1)}, bf16[20,8,2048]{2,1,0:T(8,128)(2,1)S(1)}, u32[]{:S(2)}, u32[]{:S(2)}) %collective-permute-start.6) | collective-permute-done | bytes 655392 | tf_op jit(solution)/shard_map/ppermute | solution.py:42
  148.5 2.7 %collective-permute-start.8 = (bf16[10,8,2048]{2,0,1:T(8,128)(2,1)S(1)}, bf16[10,8,2048]{2,0,1:T(8,128)(2,1)S(1)}, u32[]{:S(2)}, u32[]{:S(2)}) collective-permute-start(bf16[10,8,2048]{2,0,1:T(8,128)(2,1)S(1)} %copy.155), channel_id=1, source_target_pairs={{0,6},{2,0},{4,2},{6,4},{1,7},{3,1},{5,3},{7,5},{8,14},{10,8},{12,... | collective-permute-start | bytes 983048 | tf_op jit(solution)/shard_map/ppermute | solution.py:47
  152.0 10.3 %collective-permute-done.7 = bf16[10,8,2048]{2,0,1:T(8,128)(2,1)S(1)} collective-permute-done((bf16[10,8,2048]{2,0,1:T(8,128)(2,1)S(1)}, bf16[10,8,2048]{2,0,1:T(8,128)(2,1)S(1)}, u32[]{:S(2)}, u32[]{:S(2)}) %collective-permute-start.7) | collective-permute-done | bytes 327712 | tf_op jit(solution)/shard_map/ppermute | solution.py:42
  167.3 6.9 %fusion = f32[640,2,704]{0,2,1:T(8,128)S(1)} fusion(bf16[640,2048,1]{1,0,2:T(8,128)(2,1)S(1)} %bitcast.157, bf16[2048,2,704]{0,2,1:T(8,128)(2,1)} %bitcast.164), kind=kOutput, calls=%fused_computation | convolution fusion | flops 3690987520 | bytes 11993088 | tf_op jit(solution)/shard_map/dot_general | solution.py:165
  174.2 2.3 convolution_convert_fusion.1
  176.6 6.8 %fusion.57 = f32[640,2,704]{0,2,1:T(8,128)S(1)} fusion(bf16[640,2048,1]{1,0,2:T(8,128)(2,1)S(1)} %bitcast.158, bf16[2,704,2048]{2,1,0:T(8,128)(2,1)} %bitcast.34), kind=kOutput, calls=%fused_computation.110 | convolution fusion | flops 3690987520 | bytes 11993088 | tf_op jit(solution)/shard_map/dot_general | solution.py:165
  183.3 2.4 fusion.56
  186.2 3.1 %collective-permute-start.11 = (bf16[80,2048]{1,0:T(8,128)(2,1)S(1)}, bf16[80,2048]{1,0:T(8,128)(2,1)S(1)}, u32[]{:S(2)}, u32[]{:S(2)}) collective-permute-start(bf16[80,2048]{1,0:T(8,128)(2,1)S(1)} %get-tuple-element.17), channel_id=1, source_target_pairs={{0,6},{2,0},{4,2},{6,4},{1,7},{3,1},{5,3},{7,5},{8,14},{10,8},{12,... | collective-permute-start | bytes 983048 | tf_op jit(solution)/shard_map/ppermute | solution.py:47
  189.3 7.1 %collective-permute-done.11 = bf16[80,2048]{1,0:T(8,128)(2,1)S(1)} collective-permute-done((bf16[80,2048]{1,0:T(8,128)(2,1)S(1)}, bf16[80,2048]{1,0:T(8,128)(2,1)S(1)}, u32[]{:S(2)}, u32[]{:S(2)}) %collective-permute-start.11) | collective-permute-done | bytes 327712 | tf_op jit(solution)/shard_map/ppermute | solution.py:47
  196.4 3.1 %collective-permute-done.13 = bf16[80,2048]{1,0:T(8,128)(2,1)S(1)} collective-permute-done((bf16[80,2048]{1,0:T(8,128)(2,1)S(1)}, bf16[80,2048]{1,0:T(8,128)(2,1)S(1)}, u32[]{:S(2)}, u32[]{:S(2)}) %collective-permute-start.13) | collective-permute-done | bytes 327712 | tf_op jit(solution)/shard_map/ppermute | solution.py:42
  201.6 13.5 %collective-permute-done.12 = bf16[160,2048]{1,0:T(8,128)(2,1)S(1)} collective-permute-done((bf16[160,2048]{1,0:T(8,128)(2,1)S(1)}, bf16[160,2048]{1,0:T(8,128)(2,1)S(1)}, u32[]{:S(2)}, u32[]{:S(2)}) %collective-permute-start.12) | collective-permute-done | bytes 655392 | tf_op jit(solution)/shard_map/ppermute | solution.py:47
  218.4 3.5 %all-to-all-start.3 = ((bf16[20,8,2048]{2,0,1:T(8,128)(2,1)}), bf16[20,8,2048]{2,0,1:T(8,128)(2,1)S(1)}, u32[]{:S(2)}, u32[]{:S(2)}) async-start(bf16[20,8,2048]{2,0,1:T(8,128)(2,1)} %copy.141), calls=%async_computation.3 | async-start | bytes 1572864 | tf_op jit(solution)/shard_map/all_to_all | solution.py:175
  222.0 21.9 %all-to-all-done.3 = bf16[20,8,2048]{2,0,1:T(8,128)(2,1)S(1)} async-done(((bf16[20,8,2048]{2,0,1:T(8,128)(2,1)}), bf16[20,8,2048]{2,0,1:T(8,128)(2,1)S(1)}, u32[]{:S(2)}, u32[]{:S(2)}) %all-to-all-start.3) | async-done | bytes 655392 | tf_op jit(solution)/shard_map/all_to_all | solution.py:175
  (120 shorter events, 36.4 us)
Async XLA Ops:
  6.5 38.5 %all-gather.4.cloned.1.call-start = ((), (), s32[]{:S(2)}) async-start(), calls=%async_computation.4 | async-start | bytes 1310720 | tf_op jit(solution)/shard_map/all_gather | solution.py:101
  7.3 116.4 %all-gather.6.cloned.1.call-start = ((), (), s32[]{:S(2)}) async-start(), calls=%async_computation.5 | async-start | bytes 7208960 | tf_op jit(solution)/shard_map/all_gather | solution.py:102
  42.1 15.2 %collective-permute-start.1 = (bf16[20,8,2048]{2,1,0:T(8,128)(2,1)S(1)}, bf16[20,8,2048]{2,1,0:T(8,128)(2,1)S(1)}, u32[]{:S(2)}, u32[]{:S(2)}) collective-permute-start(bf16[20,8,2048]{2,1,0:T(8,128)(2,1)S(1)} %copy.123), channel_id=1, source_target_pairs={{0,2},{2,4},{4,6},{6,0},{1,3},{3,5},{5,7},{7,1},{8,10},{10,12},{12... | collective-permute-start | bytes 1966088 | tf_op jit(solution)/shard_map/ppermute | solution.py:42
  43.5 13.9 %collective-permute-start = (bf16[20,8,2048]{2,1,0:T(8,128)(2,1)S(1)}, bf16[20,8,2048]{2,1,0:T(8,128)(2,1)S(1)}, u32[]{:S(2)}, u32[]{:S(2)}) collective-permute-start(bf16[20,8,2048]{2,1,0:T(8,128)(2,1)S(1)} %copy.123), channel_id=1, source_target_pairs={{0,6},{2,0},{4,2},{6,4},{1,7},{3,1},{5,3},{7,5},{8,14},{10,8},{12,... | collective-permute-start | bytes 1966088 | tf_op jit(solution)/shard_map/ppermute | solution.py:47
  45.0 20.3 %collective-permute-start.4 = (bf16[2048,256]{1,0:T(8,128)(2,1)}, bf16[2048,256]{1,0:T(8,128)(2,1)}, u32[]{:S(2)}, u32[]{:S(2)}) collective-permute-start(bf16[2048,256]{1,0:T(8,128)(2,1)} %bitcast.167), channel_id=1, source_target_pairs={{0,1},{1,0},{2,3},{3,2},{4,5},{5,4},{6,7},{7,6},{8,9},{9,8},{10,11... | collective-permute-start | bytes 3145736 | tf_op jit(solution)/shard_map/ppermute | solution.py:76
  57.3 7.6 %collective-permute-start.2 = (bf16[10,8,2048]{2,1,0:T(8,128)(2,1)S(1)}, bf16[10,8,2048]{2,1,0:T(8,128)(2,1)S(1)}, u32[]{:S(2)}, u32[]{:S(2)}) collective-permute-start(bf16[10,8,2048]{2,1,0:T(8,128)(2,1)S(1)} %slice.100), channel_id=1, source_target_pairs={{0,2},{2,4},{4,6},{6,0},{1,3},{3,5},{5,7},{7,1},{8,10},{10,12},{12... | collective-permute-start | bytes 983048 | tf_op jit(solution)/shard_map/ppermute | solution.py:42
  57.5 7.5 %collective-permute-start.3 = (bf16[10,8,2048]{2,1,0:T(8,128)(2,1)S(1)}, bf16[10,8,2048]{2,1,0:T(8,128)(2,1)S(1)}, u32[]{:S(2)}, u32[]{:S(2)}) collective-permute-start(bf16[10,8,2048]{2,1,0:T(8,128)(2,1)S(1)} %slice.101), channel_id=1, source_target_pairs={{0,6},{2,0},{4,2},{6,4},{1,7},{3,1},{5,3},{7,5},{8,14},{10,8},{12,... | collective-permute-start | bytes 983048 | tf_op jit(solution)/shard_map/ppermute | solution.py:47
  71.8 26.2 %all-to-all-start.1 = ((bf16[32,20,512]{2,1,0:T(8,128)(2,1)}), bf16[32,20,512]{2,1,0:T(8,128)(2,1)S(1)}, u32[]{:S(2)}, u32[]{:S(2)}) async-start(bf16[32,20,512]{2,1,0:T(8,128)(2,1)} %bitcast.11), calls=%async_computation.1 | async-start | bytes 1572864 | tf_op jit(solution)/shard_map/all_to_all | solution.py:131
  102.0 21.7 %all-to-all-start.2 = ((bf16[20,8,2048]{2,0,1:T(8,128)(2,1)}), bf16[20,8,2048]{2,0,1:T(8,128)(2,1)S(1)}, u32[]{:S(2)}, u32[]{:S(2)}) async-start(bf16[20,8,2048]{2,0,1:T(8,128)(2,1)} %copy.133), calls=%async_computation.2 | async-start | bytes 1572864 | tf_op jit(solution)/shard_map/all_to_all | solution.py:149
  105.5 58.5 %all-gather.8.cloned.1.call-start = ((), (), s32[]{:S(2)}) async-start(), calls=%async_computation.6 | async-start | bytes 3604480 | tf_op jit(solution)/shard_map/all_gather | solution.py:103
  123.6 27.9 %copy-start.2 = (bf16[20,8,2048]{2,0,1:T(8,128)(2,1)}, bf16[20,8,2048]{2,0,1:T(8,128)(2,1)S(1)}, u32[]{:S(2)}) copy-start(bf16[20,8,2048]{2,0,1:T(8,128)(2,1)S(1)} %all-to-all-done.2) | copy-start | bytes 1966084
  123.6 52.9 %collective-permute-start.9 = (bf16[2048,1408]{0,1:T(8,128)(2,1)}, bf16[2048,1408]{0,1:T(8,128)(2,1)}, u32[]{:S(2)}, u32[]{:S(2)}) collective-permute-start(bf16[2048,1408]{0,1:T(8,128)(2,1)} %bitcast.163), channel_id=1, source_target_pairs={{0,1},{1,0},{2,3},{3,2},{4,5},{5,4},{6,7},{7,6},{8,9},{9,8},{10,11... | collective-permute-start | bytes 17301512 | tf_op jit(solution)/shard_map/ppermute | solution.py:76
  130.0 17.9 %collective-permute-start.6 = (bf16[20,8,2048]{2,1,0:T(8,128)(2,1)S(1)}, bf16[20,8,2048]{2,1,0:T(8,128)(2,1)S(1)}, u32[]{:S(2)}, u32[]{:S(2)}) collective-permute-start(bf16[20,8,2048]{2,1,0:T(8,128)(2,1)S(1)} %copy.134), channel_id=1, source_target_pairs={{0,2},{2,4},{4,6},{6,0},{1,3},{3,5},{5,7},{7,1},{8,10},{10,12},{12... | collective-permute-start | bytes 1966088 | tf_op jit(solution)/shard_map/ppermute | solution.py:42
  131.5 16.8 %collective-permute-start.5 = (bf16[20,8,2048]{2,1,0:T(8,128)(2,1)S(1)}, bf16[20,8,2048]{2,1,0:T(8,128)(2,1)S(1)}, u32[]{:S(2)}, u32[]{:S(2)}) collective-permute-start(bf16[20,8,2048]{2,1,0:T(8,128)(2,1)S(1)} %copy.134), channel_id=1, source_target_pairs={{0,6},{2,0},{4,2},{6,4},{1,7},{3,1},{5,3},{7,5},{8,14},{10,8},{12,... | collective-permute-start | bytes 1966088 | tf_op jit(solution)/shard_map/ppermute | solution.py:47
  148.1 14.2 %collective-permute-start.7 = (bf16[10,8,2048]{2,0,1:T(8,128)(2,1)S(1)}, bf16[10,8,2048]{2,0,1:T(8,128)(2,1)S(1)}, u32[]{:S(2)}, u32[]{:S(2)}) collective-permute-start(bf16[10,8,2048]{2,0,1:T(8,128)(2,1)S(1)} %copy.156), channel_id=1, source_target_pairs={{0,2},{2,4},{4,6},{6,0},{1,3},{3,5},{5,7},{7,1},{8,10},{10,12},{12... | collective-permute-start | bytes 983048 | tf_op jit(solution)/shard_map/ppermute | solution.py:42
  148.5 13.8 %collective-permute-start.8 = (bf16[10,8,2048]{2,0,1:T(8,128)(2,1)S(1)}, bf16[10,8,2048]{2,0,1:T(8,128)(2,1)S(1)}, u32[]{:S(2)}, u32[]{:S(2)}) collective-permute-start(bf16[10,8,2048]{2,0,1:T(8,128)(2,1)S(1)} %copy.155), channel_id=1, source_target_pairs={{0,6},{2,0},{4,2},{6,4},{1,7},{3,1},{5,3},{7,5},{8,14},{10,8},{12,... | collective-permute-start | bytes 983048 | tf_op jit(solution)/shard_map/ppermute | solution.py:47
  164.1 19.3 %collective-permute-start.10 = (bf16[704,2048]{1,0:T(8,128)(2,1)}, bf16[704,2048]{1,0:T(8,128)(2,1)S(1)}, u32[]{:S(2)}, u32[]{:S(2)}) collective-permute-start(bf16[704,2048]{1,0:T(8,128)(2,1)} %bitcast.165), channel_id=1, source_target_pairs={{0,1},{1,0},{2,3},{3,2},{4,5},{5,4},{6,7},{7,6},{8,9},{9,8},{10,11... | collective-permute-start | bytes 8650760 | tf_op jit(solution)/shard_map/ppermute | solution.py:76
  186.2 10.2 %collective-permute-start.11 = (bf16[80,2048]{1,0:T(8,128)(2,1)S(1)}, bf16[80,2048]{1,0:T(8,128)(2,1)S(1)}, u32[]{:S(2)}, u32[]{:S(2)}) collective-permute-start(bf16[80,2048]{1,0:T(8,128)(2,1)S(1)} %get-tuple-element.17), channel_id=1, source_target_pairs={{0,6},{2,0},{4,2},{6,4},{1,7},{3,1},{5,3},{7,5},{8,14},{10,8},{12,... | collective-permute-start | bytes 983048 | tf_op jit(solution)/shard_map/ppermute | solution.py:47
  189.2 10.2 %collective-permute-start.13 = (bf16[80,2048]{1,0:T(8,128)(2,1)S(1)}, bf16[80,2048]{1,0:T(8,128)(2,1)S(1)}, u32[]{:S(2)}, u32[]{:S(2)}) collective-permute-start(bf16[80,2048]{1,0:T(8,128)(2,1)S(1)} %get-tuple-element.18), channel_id=1, source_target_pairs={{0,2},{2,4},{4,6},{6,0},{1,3},{3,5},{5,7},{7,1},{8,10},{10,12},{12... | collective-permute-start | bytes 983048 | tf_op jit(solution)/shard_map/ppermute | solution.py:42
  199.7 15.5 %collective-permute-start.12 = (bf16[160,2048]{1,0:T(8,128)(2,1)S(1)}, bf16[160,2048]{1,0:T(8,128)(2,1)S(1)}, u32[]{:S(2)}, u32[]{:S(2)}) collective-permute-start(bf16[160,2048]{1,0:T(8,128)(2,1)S(1)} %pad_maximum_fusion.3), channel_id=1, source_target_pairs={{0,6},{2,0},{4,2},{6,4},{1,7},{3,1},{5,3},{7,5},{8,14},{10,8},{12,... | collective-permute-start | bytes 1966088 | tf_op jit(solution)/shard_map/ppermute | solution.py:47
  200.4 21.6 %copy-start.8 = (f32[64,8]{0,1:T(8,128)S(1)}, f32[64,8]{0,1:T(8,128)}, u32[]{:S(2)}) copy-start(f32[64,8]{0,1:T(8,128)} %param.16) | copy-start | bytes 6148
  200.4 16.4 %collective-permute-start.14 = (bf16[160,2048]{1,0:T(8,128)(2,1)S(1)}, bf16[160,2048]{1,0:T(8,128)(2,1)S(1)}, u32[]{:S(2)}, u32[]{:S(2)}) collective-permute-start(bf16[160,2048]{1,0:T(8,128)(2,1)S(1)} %pad_maximum_fusion.4), channel_id=1, source_target_pairs={{0,2},{2,4},{4,6},{6,0},{1,3},{3,5},{5,7},{7,1},{8,10},{10,12},{12... | collective-permute-start | bytes 1966088 | tf_op jit(solution)/shard_map/ppermute | solution.py:42
  217.1 27.7 %copy-start.1 = (f32[64,2048]{1,0:T(8,128)S(1)}, f32[64,2048]{1,0:T(8,128)}, u32[]{:S(2)}) copy-start(f32[64,2048]{1,0:T(8,128)} %copy-done) | copy-start | bytes 1572868
  218.4 25.5 %all-to-all-start.3 = ((bf16[20,8,2048]{2,0,1:T(8,128)(2,1)}), bf16[20,8,2048]{2,0,1:T(8,128)(2,1)S(1)}, u32[]{:S(2)}, u32[]{:S(2)}) async-start(bf16[20,8,2048]{2,0,1:T(8,128)(2,1)} %copy.141), calls=%async_computation.3 | async-start | bytes 1572864 | tf_op jit(solution)/shard_map/all_to_all | solution.py:175
  (9 other events, 91.1 us)
Sparse Core Ops, SparseCore 0:
  9.2 29.3 all-gather.3
  40.4 65.0 all-gather.5
  108.2 45.6 all-gather.7

commit v2 on v1

--- a/solution.py
+++ b/solution.py
@@ -153,10 +153,14 @@
         concat_axis=1,
         tiled=True,
     )
-    gate_matrix, _ = lax.optimization_barrier((gate_matrix, arrived))
+    half = capacity // 2
+    left = from_left(arrived)
+    right = from_right(arrived)
+    gate_matrix, _, _ = lax.optimization_barrier((gate_matrix, left, right))
     depth = gate_matrix.shape[0]
     gate_own, gate_other = chip_pair(gate_matrix.reshape(depth, 2 * hid_slice))
-    incoming = ring_copies(arrived)
+    far = jnp.concatenate([from_left(left[:half]), from_right(right[half:])], axis=0)
+    incoming = jnp.stack([arrived, right, far, left], axis=0)
     flattened = incoming.reshape(-1, model_width)
     down_matrix, _ = lax.optimization_barrier((down_matrix, incoming))
     down_own, down_other = chip_pair(down_matrix)

time: 254 us -> 257 us (1.012)
  blocking collectives: 30.4 us -> 51.3 us
  waiting for transfers between devices: 123 us -> 108 us
    all_to_all x0 -> x1, blocking collectives: none -> 20.9 us  [local(): lax.all_to_all(outgoing_rows.reshape(capacity, EXPERTS, model_width), 'ez...]
    all_to_all x1 -> x0, waiting for transfers between devices: 17.4 us -> none  [local(): lax.all_to_all(outgoing_rows.reshape(capacity, EXPERTS, model_width), 'ez...]
    ppermute x6, waiting for transfers between devices: 44 us -> 32.9 us  [from_left(): return lax.ppermute(x, 'ey', [(i, (i + 1) % n) for i in range(n)])]
    ppermute x6, waiting for transfers between devices: 20.6 us -> 28.8 us  [from_right(): return lax.ppermute(x, 'ey', [(i, (i - 1) % n) for i in range(n)])]
    all_gather x1, waiting for transfers between devices: 0.02 us -> 6.28 us  [local(): down_matrix = lax.all_gather(ffn_down, 'dp', axis=2, tiled=True)[0]]
    all_to_all x1 -> x0, starting transfers between devices: 3.55 us -> none  [local(): lax.all_to_all(outgoing_rows.reshape(capacity, EXPERTS, model_width), 'ez...]
    all_to_all x1, starting transfers between devices: 3.55 us -> 6.74 us  [local(): lax.all_to_all(reduced, 'ez', split_axis=1, concat_axis=1, tiled=True)]
  transfers between devices with their start and end apart: 21 -> 20, of which waited for: 11 -> 12; matrix products, arithmetic and copies ran while one was open for 14% -> 13% of each run, Pallas kernels for 0% -> 0%
where the time goes in v2:
time: 257 us; the launch traced here: 256 us
  waiting for transfers between devices  108 us (42%)
  blocking collectives  51.3 us (20%)
  starting transfers between devices  41.7 us (16%)
  matrix products  23.3 us (9%)
  between operations  13.7 us (5%)
  local copies, waits for them, and re-layouts  12.4 us (5%)
  other arithmetic  5.79 us (2%)
    ppermute x6, waiting for transfers between devices, from_left(): return lax.ppermute(x, 'ey', [(i, (i + 1) % n) for i in range(n)])  32.9 us
    all_to_all x1, blocking collectives, dispatch(): lax.all_to_all(blocks, 'ez', split_axis=1, concat_axis=1, tiled=True)  30.4 us
    ppermute x6, waiting for transfers between devices, from_right(): return lax.ppermute(x, 'ey', [(i, (i - 1) % n) for i in range(n)])  28.8 us
    all_to_all x1, waiting for transfers between devices, local(): lax.all_to_all(reduced, 'ez', split_axis=1, concat_axis=1, tiled=True)  21.6 us
    all_to_all x1, blocking collectives, local(): lax.all_to_all(outgoing_rows.reshape(capacity, EXPERTS, model_width), 'ez...  20.9 us
    all_to_all x1, waiting for transfers between devices, local(): lax.all_to_all(mapped, ('ez', 'ey'), split_axis=0, concat_axis=0, tiled=T...  16.9 us
    dot_general x2, matrix products, slice_part(): gate_up = jnp.dot(flattened, gate_w, preferred_element_type=jnp.float32)  13.7 us
    ppermute x6, starting transfers between devices, from_right(): return lax.ppermute(x, 'ey', [(i, (i - 1) % n) for i in range(n)])  13.6 us
  transfers between devices with their start and end apart: 20, of which 12 were waited for; matrix products, arithmetic and copies ran while one was open for 13% of the time, Pallas kernels for 0%

profile of v2, /device:TPU:1, one launch (start us, length us, event | category | flops | bytes accessed | tf_op | source)
XLA Modules:
  0.0 256.1 jit_solution(15885508468907276389)
XLA Ops:
  11.3 30.4 %all_to_all.20 = bf16[20,8,2048]{2,0,1:T(8,128)(2,1)S(1)} all-to-all(bf16[20,8,2048]{2,0,1:T(8,128)(2,1)S(1)} %copy.122), channel_id=1, replica_groups=mesh['dp'=4,'ez'=8,'ey'=4,'ec'=2] {'ez'}, dimensions={1} | all-to-all | bytes 1310720 | tf_op jit(solution)/shard_map/all_to_all | solution.py:71
  45.0 2.9 %collective-permute-start.4 = (bf16[2048,256]{1,0:T(8,128)(2,1)}, bf16[2048,256]{1,0:T(8,128)(2,1)}, u32[]{:S(2)}, u32[]{:S(2)}) collective-permute-start(bf16[2048,256]{1,0:T(8,128)(2,1)} %bitcast.167), channel_id=1, source_target_pairs={{0,1},{1,0},{2,3},{3,2},{4,5},{5,4},{6,7},{7,6},{8,9},{9,8},{10,11... | collective-permute-start | bytes 3145736 | tf_op jit(solution)/shard_map/ppermute | solution.py:76
  47.9 9.4 %collective-permute-done.1 = bf16[20,8,2048]{2,1,0:T(8,128)(2,1)S(1)} collective-permute-done((bf16[20,8,2048]{2,1,0:T(8,128)(2,1)S(1)}, bf16[20,8,2048]{2,1,0:T(8,128)(2,1)S(1)}, u32[]{:S(2)}, u32[]{:S(2)}) %collective-permute-start.1) | collective-permute-done | bytes 655392 | tf_op jit(solution)/shard_map/ppermute | solution.py:42
  57.5 2.7 %collective-permute-start.3 = (bf16[10,8,2048]{2,1,0:T(8,128)(2,1)S(1)}, bf16[10,8,2048]{2,1,0:T(8,128)(2,1)S(1)}, u32[]{:S(2)}, u32[]{:S(2)}) collective-permute-start(bf16[10,8,2048]{2,1,0:T(8,128)(2,1)S(1)} %slice.101), channel_id=1, source_target_pairs={{0,6},{2,0},{4,2},{6,4},{1,7},{3,1},{5,3},{7,5},{8,14},{10,8},{12,... | collective-permute-start | bytes 983048 | tf_op jit(solution)/shard_map/ppermute | solution.py:47
  60.6 4.4 %collective-permute-done.2 = bf16[10,8,2048]{2,1,0:T(8,128)(2,1)S(1)} collective-permute-done((bf16[10,8,2048]{2,1,0:T(8,128)(2,1)S(1)}, bf16[10,8,2048]{2,1,0:T(8,128)(2,1)S(1)}, u32[]{:S(2)}, u32[]{:S(2)}) %collective-permute-start.2) | collective-permute-done | bytes 327712 | tf_op jit(solution)/shard_map/ppermute | solution.py:42
  71.9 7.8 %all-to-all-start.1 = ((bf16[32,20,512]{2,1,0:T(8,128)(2,1)}), bf16[32,20,512]{2,1,0:T(8,128)(2,1)S(1)}, u32[]{:S(2)}, u32[]{:S(2)}) async-start(bf16[32,20,512]{2,1,0:T(8,128)(2,1)} %bitcast.11), calls=%async_computation.1 | async-start | bytes 1572864 | tf_op jit(solution)/shard_map/all_to_all | solution.py:131
  81.1 16.9 %all-to-all-done.1 = bf16[32,20,512]{2,1,0:T(8,128)(2,1)S(1)} async-done(((bf16[32,20,512]{2,1,0:T(8,128)(2,1)}), bf16[32,20,512]{2,1,0:T(8,128)(2,1)S(1)}, u32[]{:S(2)}, u32[]{:S(2)}) %all-to-all-start.1) | async-done | bytes 655392 | tf_op jit(solution)/shard_map/all_to_all | solution.py:131
  100.3 20.9 %all_to_all.21 = bf16[20,8,2048]{2,0,1:T(8,128)(2,1)S(1)} all-to-all(bf16[20,8,2048]{2,0,1:T(8,128)(2,1)S(1)} %copy.133), channel_id=1, replica_groups=mesh['dp'=4,'ez'=8,'ey'=4,'ec'=2] {'ez'}, dimensions={1} | all-to-all | bytes 1310720 | tf_op jit(solution)/shard_map/all_to_all | solution.py:149
  121.6 3.4 %collective-permute-start.5 = (bf16[20,8,2048]{2,1,0:T(8,128)(2,1)S(1)}, bf16[20,8,2048]{2,1,0:T(8,128)(2,1)S(1)}, u32[]{:S(2)}, u32[]{:S(2)}) collective-permute-start(bf16[20,8,2048]{2,1,0:T(8,128)(2,1)S(1)} %copy.134), channel_id=1, source_target_pairs={{0,6},{2,0},{4,2},{6,4},{1,7},{3,1},{5,3},{7,5},{8,14},{10,8},{12,... | collective-permute-start | bytes 1966088 | tf_op jit(solution)/shard_map/ppermute | solution.py:47
  125.0 8.2 %collective-permute-done.5 = bf16[20,8,2048]{2,1,0:T(8,128)(2,1)S(1)} collective-permute-done((bf16[20,8,2048]{2,1,0:T(8,128)(2,1)S(1)}, bf16[20,8,2048]{2,1,0:T(8,128)(2,1)S(1)}, u32[]{:S(2)}, u32[]{:S(2)}) %collective-permute-start.5) | collective-permute-done | bytes 655392 | tf_op jit(solution)/shard_map/ppermute | solution.py:47
  133.2 3.1 %collective-permute-done.6 = bf16[20,8,2048]{2,1,0:T(8,128)(2,1)S(1)} collective-permute-done((bf16[20,8,2048]{2,1,0:T(8,128)(2,1)S(1)}, bf16[20,8,2048]{2,1,0:T(8,128)(2,1)S(1)}, u32[]{:S(2)}, u32[]{:S(2)}) %collective-permute-start.6) | collective-permute-done | bytes 655392 | tf_op jit(solution)/shard_map/ppermute | solution.py:42
  136.3 7.0 %collective-permute-start.9 = (bf16[2048,1408]{0,1:T(8,128)(2,1)}, bf16[2048,1408]{0,1:T(8,128)(2,1)}, u32[]{:S(2)}, u32[]{:S(2)}) collective-permute-start(bf16[2048,1408]{0,1:T(8,128)(2,1)} %bitcast.163), channel_id=1, source_target_pairs={{0,1},{1,0},{2,3},{3,2},{4,5},{5,4},{6,7},{7,6},{8,9},{9,8},{10,11... | collective-permute-start | bytes 17301512 | tf_op jit(solution)/shard_map/ppermute | solution.py:76
  143.9 2.7 %collective-permute-start.8 = (bf16[10,8,2048]{2,0,1:T(8,128)(2,1)S(1)}, bf16[10,8,2048]{2,0,1:T(8,128)(2,1)S(1)}, u32[]{:S(2)}, u32[]{:S(2)}) collective-permute-start(bf16[10,8,2048]{2,0,1:T(8,128)(2,1)S(1)} %copy.155), channel_id=1, source_target_pairs={{0,6},{2,0},{4,2},{6,4},{1,7},{3,1},{5,3},{7,5},{8,14},{10,8},{12,... | collective-permute-start | bytes 983048 | tf_op jit(solution)/shard_map/ppermute | solution.py:47
  147.4 11.1 %collective-permute-done.7 = bf16[10,8,2048]{2,0,1:T(8,128)(2,1)S(1)} collective-permute-done((bf16[10,8,2048]{2,0,1:T(8,128)(2,1)S(1)}, bf16[10,8,2048]{2,0,1:T(8,128)(2,1)S(1)}, u32[]{:S(2)}, u32[]{:S(2)}) %collective-permute-start.7) | collective-permute-done | bytes 327712 | tf_op jit(solution)/shard_map/ppermute | solution.py:42
  160.2 6.3 %all-gather.8.cloned.1.call-done = bf16[1,704,2048]{2,1,0:T(8,128)(2,1)} async-done(((bf16[1,704,512]{2,1,0:T(8,128)(2,1)}), bf16[1,704,2048]{2,1,0:T(8,128)(2,1)}) %all-gather.8.cloned.1.call-update) | async-done | bytes 2883600 | tf_op jit(solution)/shard_map/all_gather | solution.py:103
  168.7 6.9 %fusion = f32[640,2,704]{0,2,1:T(8,128)S(1)} fusion(bf16[640,2048,1]{1,0,2:T(8,128)(2,1)S(1)} %bitcast.157, bf16[2048,2,704]{0,2,1:T(8,128)(2,1)} %bitcast.164), kind=kOutput, calls=%fused_computation | convolution fusion | flops 3690987520 | bytes 11993088 | tf_op jit(solution)/shard_map/dot_general | solution.py:169
  177.9 6.8 %fusion.57 = f32[640,2,704]{0,2,1:T(8,128)S(1)} fusion(bf16[640,2048,1]{1,0,2:T(8,128)(2,1)S(1)} %bitcast.158, bf16[2,704,2048]{2,1,0:T(8,128)(2,1)} %bitcast.34), kind=kOutput, calls=%fused_computation.110 | convolution fusion | flops 3690987520 | bytes 11993088 | tf_op jit(solution)/shard_map/dot_general | solution.py:169
  184.7 2.4 fusion.56
  187.6 2.5 collective-permute-start.11
  190.2 7.1 %collective-permute-done.11 = bf16[80,2048]{1,0:T(8,128)(2,1)S(1)} collective-permute-done((bf16[80,2048]{1,0:T(8,128)(2,1)S(1)}, bf16[80,2048]{1,0:T(8,128)(2,1)S(1)}, u32[]{:S(2)}, u32[]{:S(2)}) %collective-permute-start.11) | collective-permute-done | bytes 327712 | tf_op jit(solution)/shard_map/ppermute | solution.py:47
  197.2 3.1 %collective-permute-done.13 = bf16[80,2048]{1,0:T(8,128)(2,1)S(1)} collective-permute-done((bf16[80,2048]{1,0:T(8,128)(2,1)S(1)}, bf16[80,2048]{1,0:T(8,128)(2,1)S(1)}, u32[]{:S(2)}, u32[]{:S(2)}) %collective-permute-start.13) | collective-permute-done | bytes 327712 | tf_op jit(solution)/shard_map/ppermute | solution.py:42
  202.5 13.5 %collective-permute-done.12 = bf16[160,2048]{1,0:T(8,128)(2,1)S(1)} collective-permute-done((bf16[160,2048]{1,0:T(8,128)(2,1)S(1)}, bf16[160,2048]{1,0:T(8,128)(2,1)S(1)}, u32[]{:S(2)}, u32[]{:S(2)}) %collective-permute-start.12) | collective-permute-done | bytes 655392 | tf_op jit(solution)/shard_map/ppermute | solution.py:47
  219.3 6.7 %all-to-all-start.3 = ((bf16[20,8,2048]{2,0,1:T(8,128)(2,1)}), bf16[20,8,2048]{2,0,1:T(8,128)(2,1)S(1)}, u32[]{:S(2)}, u32[]{:S(2)}) async-start(bf16[20,8,2048]{2,0,1:T(8,128)(2,1)} %copy.141), calls=%async_computation.3 | async-start | bytes 1572864 | tf_op jit(solution)/shard_map/all_to_all | solution.py:179
  226.1 21.6 %all-to-all-done.3 = bf16[20,8,2048]{2,0,1:T(8,128)(2,1)S(1)} async-done(((bf16[20,8,2048]{2,0,1:T(8,128)(2,1)}), bf16[20,8,2048]{2,0,1:T(8,128)(2,1)S(1)}, u32[]{:S(2)}, u32[]{:S(2)}) %all-to-all-start.3) | async-done | bytes 655392 | tf_op jit(solution)/shard_map/all_to_all | solution.py:179
  (119 shorter events, 34.6 us)
Async XLA Ops:
  6.5 38.5 %all-gather.4.cloned.1.call-start = ((), (), s32[]{:S(2)}) async-start(), calls=%async_computation.4 | async-start | bytes 1310720 | tf_op jit(solution)/shard_map/all_gather | solution.py:101
  7.3 129.0 %all-gather.6.cloned.1.call-start = ((), (), s32[]{:S(2)}) async-start(), calls=%async_computation.5 | async-start | bytes 7208960 | tf_op jit(solution)/shard_map/all_gather | solution.py:102
  42.1 15.2 %collective-permute-start.1 = (bf16[20,8,2048]{2,1,0:T(8,128)(2,1)S(1)}, bf16[20,8,2048]{2,1,0:T(8,128)(2,1)S(1)}, u32[]{:S(2)}, u32[]{:S(2)}) collective-permute-start(bf16[20,8,2048]{2,1,0:T(8,128)(2,1)S(1)} %copy.123), channel_id=1, source_target_pairs={{0,2},{2,4},{4,6},{6,0},{1,3},{3,5},{5,7},{7,1},{8,10},{10,12},{12... | collective-permute-start | bytes 1966088 | tf_op jit(solution)/shard_map/ppermute | solution.py:42
  43.5 13.9 %collective-permute-start = (bf16[20,8,2048]{2,1,0:T(8,128)(2,1)S(1)}, bf16[20,8,2048]{2,1,0:T(8,128)(2,1)S(1)}, u32[]{:S(2)}, u32[]{:S(2)}) collective-permute-start(bf16[20,8,2048]{2,1,0:T(8,128)(2,1)S(1)} %copy.123), channel_id=1, source_target_pairs={{0,6},{2,0},{4,2},{6,4},{1,7},{3,1},{5,3},{7,5},{8,14},{10,8},{12,... | collective-permute-start | bytes 1966088 | tf_op jit(solution)/shard_map/ppermute | solution.py:47
  45.0 20.3 %collective-permute-start.4 = (bf16[2048,256]{1,0:T(8,128)(2,1)}, bf16[2048,256]{1,0:T(8,128)(2,1)}, u32[]{:S(2)}, u32[]{:S(2)}) collective-permute-start(bf16[2048,256]{1,0:T(8,128)(2,1)} %bitcast.167), channel_id=1, source_target_pairs={{0,1},{1,0},{2,3},{3,2},{4,5},{5,4},{6,7},{7,6},{8,9},{9,8},{10,11... | collective-permute-start | bytes 3145736 | tf_op jit(solution)/shard_map/ppermute | solution.py:76
  57.3 7.6 %collective-permute-start.2 = (bf16[10,8,2048]{2,1,0:T(8,128)(2,1)S(1)}, bf16[10,8,2048]{2,1,0:T(8,128)(2,1)S(1)}, u32[]{:S(2)}, u32[]{:S(2)}) collective-permute-start(bf16[10,8,2048]{2,1,0:T(8,128)(2,1)S(1)} %slice.100), channel_id=1, source_target_pairs={{0,2},{2,4},{4,6},{6,0},{1,3},{3,5},{5,7},{7,1},{8,10},{10,12},{12... | collective-permute-start | bytes 983048 | tf_op jit(solution)/shard_map/ppermute | solution.py:42
  57.5 7.5 %collective-permute-start.3 = (bf16[10,8,2048]{2,1,0:T(8,128)(2,1)S(1)}, bf16[10,8,2048]{2,1,0:T(8,128)(2,1)S(1)}, u32[]{:S(2)}, u32[]{:S(2)}) collective-permute-start(bf16[10,8,2048]{2,1,0:T(8,128)(2,1)S(1)} %slice.101), channel_id=1, source_target_pairs={{0,6},{2,0},{4,2},{6,4},{1,7},{3,1},{5,3},{7,5},{8,14},{10,8},{12,... | collective-permute-start | bytes 983048 | tf_op jit(solution)/shard_map/ppermute | solution.py:47
  71.9 26.2 %all-to-all-start.1 = ((bf16[32,20,512]{2,1,0:T(8,128)(2,1)}), bf16[32,20,512]{2,1,0:T(8,128)(2,1)S(1)}, u32[]{:S(2)}, u32[]{:S(2)}) async-start(bf16[32,20,512]{2,1,0:T(8,128)(2,1)} %bitcast.11), calls=%async_computation.1 | async-start | bytes 1572864 | tf_op jit(solution)/shard_map/all_to_all | solution.py:131
  79.6 86.9 %all-gather.8.cloned.1.call-start = ((), (), s32[]{:S(2)}) async-start(), calls=%async_computation.6 | async-start | bytes 3604480 | tf_op jit(solution)/shard_map/all_gather | solution.py:103
  121.2 25.8 %copy-start.2 = (bf16[20,8,2048]{2,0,1:T(8,128)(2,1)}, bf16[20,8,2048]{2,0,1:T(8,128)(2,1)S(1)}, u32[]{:S(2)}) copy-start(bf16[20,8,2048]{2,0,1:T(8,128)(2,1)S(1)} %all_to_all.21) | copy-start | bytes 1966084
  121.6 11.6 %collective-permute-start.5 = (bf16[20,8,2048]{2,1,0:T(8,128)(2,1)S(1)}, bf16[20,8,2048]{2,1,0:T(8,128)(2,1)S(1)}, u32[]{:S(2)}, u32[]{:S(2)}) collective-permute-start(bf16[20,8,2048]{2,1,0:T(8,128)(2,1)S(1)} %copy.134), channel_id=1, source_target_pairs={{0,6},{2,0},{4,2},{6,4},{1,7},{3,1},{5,3},{7,5},{8,14},{10,8},{12,... | collective-permute-start | bytes 1966088 | tf_op jit(solution)/shard_map/ppermute | solution.py:47
  125.0 11.3 %collective-permute-start.6 = (bf16[20,8,2048]{2,1,0:T(8,128)(2,1)S(1)}, bf16[20,8,2048]{2,1,0:T(8,128)(2,1)S(1)}, u32[]{:S(2)}, u32[]{:S(2)}) collective-permute-start(bf16[20,8,2048]{2,1,0:T(8,128)(2,1)S(1)} %copy.134), channel_id=1, source_target_pairs={{0,2},{2,4},{4,6},{6,0},{1,3},{3,5},{5,7},{7,1},{8,10},{10,12},{12... | collective-permute-start | bytes 1966088 | tf_op jit(solution)/shard_map/ppermute | solution.py:42
  136.3 41.6 %collective-permute-start.9 = (bf16[2048,1408]{0,1:T(8,128)(2,1)}, bf16[2048,1408]{0,1:T(8,128)(2,1)}, u32[]{:S(2)}, u32[]{:S(2)}) collective-permute-start(bf16[2048,1408]{0,1:T(8,128)(2,1)} %bitcast.163), channel_id=1, source_target_pairs={{0,1},{1,0},{2,3},{3,2},{4,5},{5,4},{6,7},{7,6},{8,9},{9,8},{10,11... | collective-permute-start | bytes 17301512 | tf_op jit(solution)/shard_map/ppermute | solution.py:76
  143.5 14.9 %collective-permute-start.7 = (bf16[10,8,2048]{2,0,1:T(8,128)(2,1)S(1)}, bf16[10,8,2048]{2,0,1:T(8,128)(2,1)S(1)}, u32[]{:S(2)}, u32[]{:S(2)}) collective-permute-start(bf16[10,8,2048]{2,0,1:T(8,128)(2,1)S(1)} %copy.156), channel_id=1, source_target_pairs={{0,2},{2,4},{4,6},{6,0},{1,3},{3,5},{5,7},{7,1},{8,10},{10,12},{12... | collective-permute-start | bytes 983048 | tf_op jit(solution)/shard_map/ppermute | solution.py:42
  143.9 14.6 %collective-permute-start.8 = (bf16[10,8,2048]{2,0,1:T(8,128)(2,1)S(1)}, bf16[10,8,2048]{2,0,1:T(8,128)(2,1)S(1)}, u32[]{:S(2)}, u32[]{:S(2)}) collective-permute-start(bf16[10,8,2048]{2,0,1:T(8,128)(2,1)S(1)} %copy.155), channel_id=1, source_target_pairs={{0,6},{2,0},{4,2},{6,4},{1,7},{3,1},{5,3},{7,5},{8,14},{10,8},{12,... | collective-permute-start | bytes 983048 | tf_op jit(solution)/shard_map/ppermute | solution.py:47
  166.5 18.2 %collective-permute-start.10 = (bf16[704,2048]{1,0:T(8,128)(2,1)}, bf16[704,2048]{1,0:T(8,128)(2,1)S(1)}, u32[]{:S(2)}, u32[]{:S(2)}) collective-permute-start(bf16[704,2048]{1,0:T(8,128)(2,1)} %bitcast.165), channel_id=1, source_target_pairs={{0,1},{1,0},{2,3},{3,2},{4,5},{5,4},{6,7},{7,6},{8,9},{9,8},{10,11... | collective-permute-start | bytes 8650760 | tf_op jit(solution)/shard_map/ppermute | solution.py:76
  187.6 9.7 %collective-permute-start.11 = (bf16[80,2048]{1,0:T(8,128)(2,1)S(1)}, bf16[80,2048]{1,0:T(8,128)(2,1)S(1)}, u32[]{:S(2)}, u32[]{:S(2)}) collective-permute-start(bf16[80,2048]{1,0:T(8,128)(2,1)S(1)} %get-tuple-element.17), channel_id=1, source_target_pairs={{0,6},{2,0},{4,2},{6,4},{1,7},{3,1},{5,3},{7,5},{8,14},{10,8},{12,... | collective-permute-start | bytes 983048 | tf_op jit(solution)/shard_map/ppermute | solution.py:47
  190.1 10.2 %collective-permute-start.13 = (bf16[80,2048]{1,0:T(8,128)(2,1)S(1)}, bf16[80,2048]{1,0:T(8,128)(2,1)S(1)}, u32[]{:S(2)}, u32[]{:S(2)}) collective-permute-start(bf16[80,2048]{1,0:T(8,128)(2,1)S(1)} %get-tuple-element.18), channel_id=1, source_target_pairs={{0,2},{2,4},{4,6},{6,0},{1,3},{3,5},{5,7},{7,1},{8,10},{10,12},{12... | collective-permute-start | bytes 983048 | tf_op jit(solution)/shard_map/ppermute | solution.py:42
  200.6 15.5 %collective-permute-start.12 = (bf16[160,2048]{1,0:T(8,128)(2,1)S(1)}, bf16[160,2048]{1,0:T(8,128)(2,1)S(1)}, u32[]{:S(2)}, u32[]{:S(2)}) collective-permute-start(bf16[160,2048]{1,0:T(8,128)(2,1)S(1)} %pad_maximum_fusion.3), channel_id=1, source_target_pairs={{0,6},{2,0},{4,2},{6,4},{1,7},{3,1},{5,3},{7,5},{8,14},{10,8},{12,... | collective-permute-start | bytes 1966088 | tf_op jit(solution)/shard_map/ppermute | solution.py:47
  201.3 24.7 %copy-start.6 = (bf16[2048]{0:T(1024)(128)(2,1)S(1)}, bf16[2048]{0:T(1024)(128)(2,1)}, u32[]{:S(2)}) copy-start(bf16[2048]{0:T(1024)(128)(2,1)} %param.21) | copy-start | bytes 12292
  201.3 24.8 %copy-start.8 = (f32[64,8]{0,1:T(8,128)S(1)}, f32[64,8]{0,1:T(8,128)}, u32[]{:S(2)}) copy-start(f32[64,8]{0,1:T(8,128)} %param.16) | copy-start | bytes 6148
  201.3 16.4 %collective-permute-start.14 = (bf16[160,2048]{1,0:T(8,128)(2,1)S(1)}, bf16[160,2048]{1,0:T(8,128)(2,1)S(1)}, u32[]{:S(2)}, u32[]{:S(2)}) collective-permute-start(bf16[160,2048]{1,0:T(8,128)(2,1)S(1)} %pad_maximum_fusion.4), channel_id=1, source_target_pairs={{0,2},{2,4},{4,6},{6,0},{1,3},{3,5},{5,7},{7,1},{8,10},{10,12},{12... | collective-permute-start | bytes 1966088 | tf_op jit(solution)/shard_map/ppermute | solution.py:42
  218.0 30.6 %copy-start.1 = (f32[64,2048]{1,0:T(8,128)S(1)}, f32[64,2048]{1,0:T(8,128)}, u32[]{:S(2)}) copy-start(f32[64,2048]{1,0:T(8,128)} %copy-done) | copy-start | bytes 1572868
  219.3 28.4 %all-to-all-start.3 = ((bf16[20,8,2048]{2,0,1:T(8,128)(2,1)}), bf16[20,8,2048]{2,0,1:T(8,128)(2,1)S(1)}, u32[]{:S(2)}, u32[]{:S(2)}) async-start(bf16[20,8,2048]{2,0,1:T(8,128)(2,1)} %copy.141), calls=%async_computation.3 | async-start | bytes 1572864 | tf_op jit(solution)/shard_map/all_to_all | solution.py:179
  (8 other events, 91.3 us)
Sparse Core Ops, SparseCore 0:
  9.2 29.3 all-gather.3
  40.4 65.0 all-gather.5
  125.1 41.3 all-gather.7
